TPU v7x, 256 devices: a whole 4x4x8 slice. The times are simulated.
256 devices in a mesh: dp: 16 (over y, x_hi, core), tensor: 16 (over x_lo, z).
Axes of the slice: x: 4 (x_hi: 2, x_lo: 2; x = x_hi * 2 + x_lo), y: 4, z: 8, core: 2. Of those that a mesh axis runs over, the one named last changes fastest.
Arguments:
- tokens: bfloat16 [768, 6144], P('dp', 'tensor'), may hold values from -6 to 6
- routes: int32 [768, 2], P('dp'), may hold values from 0 to 3, all different within a row; in each aligned block of 48 rows (0 to 47, 48 to 95, ...) at most 32 rows name the same one
- gate_weights: bfloat16 [768, 2], P('dp'), may hold values from 0.25 to 1
- gate_matrix: bfloat16 [16, 6144, 2048], P('dp', None, 'tensor'), may hold values from -0.078125 to 0.078125
- up_matrix: bfloat16 [16, 6144, 2048], P('dp', None, 'tensor'), may hold values from -0.078125 to 0.078125
- down_matrix: bfloat16 [16, 2048, 6144], P('dp', 'tensor'), may hold values from -0.0625 to 0.0625
- cotangent: bfloat16 [768, 6144], P('dp', 'tensor'), may hold values from -6 to 6
Outputs:
- layer_out: bfloat16 [768, 6144], P('dp', 'tensor')
- token_gradient: bfloat16 [768, 6144], P('dp', 'tensor')
- gate_gradient: bfloat16 [16, 6144, 2048], P('dp', None, 'tensor')
- up_gradient: bfloat16 [16, 6144, 2048], P('dp', None, 'tensor')
- down_gradient: bfloat16 [16, 2048, 6144], P('dp', 'tensor')
Inputs may be any that keep to these rules, and one draw needn't show every extreme that they name: `routes`: within the rows of one dp index (aligned blocks of 48 rows) no expert is named by more than 32 rows, and in some such block one expert is named by exactly 32; the two experts of a row differ.
All inputs are finite; a program needn't handle non-finite values.
Results may differ from a plain program's by a relative error of at most 0.018.
Values may be sent and summed in bfloat16 or wider, within the bound.
No kernel may reach another device: no remote copies, remote signals or barrier semaphores. Data moves between devices by JAX's collectives and lax.ppermute only.
A program may use at most 128 MiB of HBM per device.

v0:
```python
import jax
import jax.numpy as jnp
from jax import lax
from jax.experimental.layout import Layout, with_layout_constraint
from jax.sharding import Mesh, NamedSharding, PartitionSpec as P

EXPERTS = 4
CAP = 32
DP = ("y", "xhi", "core")
TN = ("xlo", "z")
SRC = ("y", "xhi")
precise = lax.Precision.HIGHEST


def slot_tables(routes, gate_weights, capacity):
    experts = jnp.arange(EXPERTS, dtype=jnp.int32)
    hit_mask = routes[:, :, None] == experts[None, None, :]
    chosen = jnp.any(hit_mask, axis=1)
    weights = jnp.sum(
        jnp.where(hit_mask, gate_weights.astype(jnp.float32)[:, :, None], jnp.float32(0.0)), axis=1
    )
    places = jnp.cumsum(chosen.astype(jnp.int32), axis=0) - 1
    columns = jnp.arange(capacity, dtype=jnp.int32)
    onehot = (places[:, :, None] == columns[None, None, :]) & chosen[:, :, None]
    return (onehot, weights)


def per_device(tokens, routes, gate_weights, gate_matrix, up_matrix, down_matrix, cotangent):
    feature_cols = tokens.shape[1]
    n_src = lax.axis_size(SRC)
    expert_span = n_src // EXPERTS
    onehot, weights = slot_tables(routes, gate_weights, CAP)
    member = onehot.astype(jnp.float32)
    scaled = member * weights[:, :, None]

    def spread(slot_table):
        widened = jnp.broadcast_to(
            slot_table[:, :, None, :], (slot_table.shape[0], EXPERTS, expert_span, CAP)
        )
        return widened.reshape(slot_table.shape[0], EXPERTS * expert_span * CAP)

    member_wide = spread(member)
    scaled_wide = spread(scaled)
    token_send = jnp.einsum(
        "tr,tc->rc", member_wide.astype(jnp.bfloat16), tokens, preferred_element_type=jnp.float32
    ).astype(jnp.bfloat16)
    grad_send = jnp.einsum(
        "tr,tc->rc", scaled_wide, cotangent.astype(jnp.float32), precision=precise
    ).astype(jnp.bfloat16)
    send = jnp.concatenate(
        [token_send.reshape(n_src, CAP, feature_cols), grad_send.reshape(n_src, CAP, feature_cols)],
        axis=1,
    )
    recv = lax.all_to_all(send, SRC, split_axis=0, concat_axis=0, tiled=True)
    mine = recv.reshape(n_src, 2, CAP, feature_cols).transpose(1, 0, 2, 3)
    mine = mine.reshape(2, n_src * CAP, feature_cols)
    mine_full = lax.all_gather(mine, TN, axis=2, tiled=True)
    pair = [(0, 1), (1, 0)]
    gate_local = gate_matrix[0]
    up_local = up_matrix[0]
    down_local = down_matrix[0]
    gu_local = jnp.concatenate([gate_local, up_local], axis=1)
    gu_other, down_other = lax.ppermute((gu_local, down_local), "core", pair)

    def forward(pre, gu_w, down_w):
        width = pre.shape[1] // 2
        gate_pre, up_pre = (pre[:, :width], pre[:, width:])
        sigmoid_gate = jax.nn.sigmoid(gate_pre)
        activated = gate_pre * sigmoid_gate
        hidden = (activated * up_pre).astype(jnp.bfloat16)
        out_t = jnp.einsum("hd,rh->dr", down_w, hidden, preferred_element_type=jnp.float32).astype(
            jnp.bfloat16
        )
        out_t = with_layout_constraint(out_t, Layout(major_to_minor=(0, 1)))
        return (gate_pre, up_pre, sigmoid_gate, activated, hidden, out_t)

    def backward(hidden_grad, gate_pre, up_pre, sigmoid_gate, activated, gu_w, down_w):
        gate_grad = (
            hidden_grad * up_pre * sigmoid_gate * (1.0 + gate_pre * (1.0 - sigmoid_gate))
        ).astype(jnp.bfloat16)
        up_grad = (hidden_grad * activated).astype(jnp.bfloat16)
        both_grad = jnp.concatenate([gate_grad, up_grad], axis=1)
        back_t = jnp.einsum(
            "dh,rh->dr", gu_w, both_grad, preferred_element_type=jnp.float32
        ).astype(jnp.bfloat16)
        back_t = with_layout_constraint(back_t, Layout(major_to_minor=(0, 1)))
        return (gate_grad, up_grad, back_t)

    rows, grads = (mine_full[0], mine_full[1])
    own_w = (gu_local, down_local)
    other_w = (gu_other, down_other)
    width = gu_local.shape[1]
    pre_both = jnp.dot(
        rows, jnp.concatenate([gu_local, gu_other], axis=1), preferred_element_type=jnp.float32
    )
    hgrad_both = jnp.einsum(
        "rd,hd->rh",
        grads,
        jnp.concatenate([down_local, down_other], axis=0),
        preferred_element_type=jnp.float32,
    )
    f_own = forward(pre_both[:, :width], *own_w)
    f_other = forward(pre_both[:, width:], *other_w)
    b_own = backward(hgrad_both[:, : width // 2], *f_own[:4], *own_w)
    b_other = backward(hgrad_both[:, width // 2 :], *f_other[:4], *other_w)
    own = jnp.concatenate([f_own[5], b_own[2]], axis=1)
    other = jnp.concatenate([f_other[5], b_other[2]], axis=1)
    summed = (own.astype(jnp.float32) + other.astype(jnp.float32)).astype(jnp.bfloat16)
    scattered = lax.psum_scatter(summed, TN, scatter_dimension=0, tiled=True)
    n_rows = f_own[5].shape[1]
    out_rows = scattered[:, :n_rows].T
    back_rows = scattered[:, n_rows:].T

    def weight_grads(f, b):
        return (
            jnp.einsum("rd,rh->dh", rows, b[0], preferred_element_type=jnp.float32),
            jnp.einsum("rd,rh->dh", rows, b[1], preferred_element_type=jnp.float32),
            jnp.einsum("rh,rd->hd", f[4], grads, preferred_element_type=jnp.float32),
        )

    w_own = weight_grads(f_own, b_own)
    w_recv = lax.ppermute(weight_grads(f_other, b_other), "core", pair)
    gate_gradient = (w_own[0] + w_recv[0]).astype(jnp.bfloat16)[None]
    up_gradient = (w_own[1] + w_recv[1]).astype(jnp.bfloat16)[None]
    down_gradient = (w_own[2] + w_recv[2]).astype(jnp.bfloat16)[None]
    done = jnp.concatenate(
        [out_rows.reshape(n_src, CAP, feature_cols), back_rows.reshape(n_src, CAP, feature_cols)],
        axis=1,
    )
    returned = lax.all_to_all(done, SRC, split_axis=0, concat_axis=0, tiled=True).astype(
        jnp.float32
    )
    returned_out = returned[:, :CAP].reshape(-1, feature_cols)
    returned_back = returned[:, CAP:].reshape(-1, feature_cols)
    layer_out = jnp.dot(
        scaled_wide, returned_out, precision=precise, preferred_element_type=jnp.float32
    ).astype(jnp.bfloat16)
    token_gradient = jnp.dot(
        member_wide, returned_back, precision=precise, preferred_element_type=jnp.float32
    ).astype(jnp.bfloat16)
    return (layer_out, token_gradient, gate_gradient, up_gradient, down_gradient)


def solution(mesh):
    sizes = dict(mesh.shape)
    sub = Mesh(mesh.devices.reshape(sizes["dp"] // 4, 2, 2, 2, sizes["tensor"] // 2), DP + TN)
    in_specs = (
        P(DP, TN),
        P(DP, None),
        P(DP, None),
        P(DP, None, TN),
        P(DP, None, TN),
        P(DP, TN, None),
        P(DP, TN),
    )
    out_specs = (P(DP, TN), P(DP, TN), P(DP, None, TN), P(DP, None, TN), P(DP, TN, None))
    placed = (
        P("dp", "tensor"),
        P("dp", "tensor"),
        P("dp", None, "tensor"),
        P("dp", None, "tensor"),
        P("dp", "tensor", None),
    )
    inner = jax.shard_map(
        per_device, mesh=sub, in_specs=in_specs, out_specs=out_specs, check_vma=False
    )

    def run(*args):
        outs = inner(*args)
        return tuple(
            (lax.with_sharding_constraint(o, NamedSharding(mesh, p)) for o, p in zip(outs, placed))
        )

    return run
```

profile of v0, /device:TPU:8, one launch (start us, length us, event | category | flops | bytes accessed | tf_op | source)
XLA Modules:
  0.0 240.8 jit_solution(1196696518437505472)
XLA Ops:
  7.2 0.0 all-gather.2.cloned.1.call-start
  7.3 0.8 fusion.32
  8.1 0.1 copy.33
  8.2 0.1 reduce_window_sum.11
  8.3 0.1 copy.34
  8.4 0.7 convert_element_type.89
  9.0 0.7 select_reduce_fusion
  9.8 0.3 convolution_convert_fusion.5
  10.1 0.9 convolution_convert_fusion.4
  11.1 15.8 %all_to_all.10 = bf16[8,64,384]{2,1,0:T(8,128)(2,1)S(1)} all-to-all(bf16[8,64,384]{2,1,0:T(8,128)(2,1)S(1)} %pad_maximum_fusion.1), channel_id=1, replica_groups=mesh['y'=4,'xhi'=2,'core'=2,'xlo'=2,'z'=8] {'y','xhi'}, dimensions={0} | all-to-all | bytes 786432 | tf_op jit(solution)/shard_map/all_to_all | solution.py:54
  27.0 0.8 copy.35
  27.8 0.0 all-gather.2.cloned.1.call-update
  27.8 0.0 reduce-scatter.2.cloned.1.call-start
  27.8 0.3 pad_maximum_fusion
  28.2 0.1 collective-permute-start
  28.3 0.5 collective-permute-start.1
  28.8 5.1 %collective-permute-done = bf16[6144,256]{1,0:T(8,128)(2,1)S(1)} collective-permute-done((bf16[6144,256]{1,0:T(8,128)(2,1)S(1)}, bf16[6144,256]{1,0:T(8,128)(2,1)S(1)}, u32[]{:S(2)}, u32[]{:S(2)}) %collective-permute-start) | collective-permute-done | bytes 3145760 | tf_op jit(solution)/shard_map/ppermute | solution.py:63
  33.9 76.6 %all-gather.2.cloned.1.call-done = bf16[2,256,6144]{2,1,0:T(8,128)(2,1)} async-done(((bf16[2,256,384]{2,1,0:T(8,128)(2,1)}), bf16[2,256,6144]{2,1,0:T(8,128)(2,1)}) %all-gather.2.cloned.1.call-update) | async-done | bytes 6291472 | tf_op jit(solution)/shard_map/all_gather | solution.py:57
  110.6 4.8 %fusion.8 = f32[256,512]{1,0:T(8,128)S(1)} fusion(bf16[6144,256]{1,0:T(8,128)(2,1)S(1)} %collective-permute-done, bf16[6144,128]{1,0:T(8,128)(2,1)} %bitcast.66, bf16[6144,128]{1,0:T(8,128)(2,1)} %bitcast.69, bf16[2,256,6144]{2,1,0:T(8,128)(2,1)} %all-gather.2.cloned.1.call-done), kind=kOutput, calls=%fused_computation.16 | convolution fusion | flops 1629487104 | bytes 9961472 | tf_op jit(solution)/shard_map/dot_general | solution.py:93
  115.4 2.9 %fusion.14 = f32[256,256]{1,0:T(8,128)S(1)} fusion(bf16[128,6144]{1,0:T(8,128)(2,1)} %collective-permute-done.1, bf16[128,6144]{1,0:T(8,128)(2,1)} %bitcast.10, bf16[2,256,6144]{2,1,0:T(8,128)(2,1)S(1)} %copy-done.2), kind=kOutput, calls=%fused_computation.25 | convolution fusion | flops 811597824 | bytes 6553600 | tf_op jit(solution)/shard_map/rd,hd->rh/dot_general | solution.py:96
  118.3 0.2 multiply_convert_fusion.1
  118.6 2.6 %fusion = bf16[6144,256]{1,0:T(8,128)(2,1)S(1)} fusion(bf16[256,128]{1,0:T(8,128)(2,1)S(1)} %get-tuple-element.10, bf16[1,128,6144]{2,1,0:T(8,128)(2,1)} %param.12), kind=kOutput, calls=%fused_computation.5 | convolution fusion | flops 404226048 | bytes 4784128 | tf_op jit(solution)/shard_map/hd,rh->dr/dot_general | solution.py:71
  121.2 1.0 convolution_convert_fusion.2
  122.3 2.4 %fusion.1 = bf16[6144,256]{1,0:T(8,128)(2,1)S(1)} fusion(bf16[256,128]{1,0:T(8,128)(2,1)S(1)} %get-tuple-element.9, bf16[128,6144]{1,0:T(8,128)(2,1)} %collective-permute-done.1), kind=kOutput, calls=%fused_computation.6 | convolution fusion | flops 404226048 | bytes 4784128 | tf_op jit(solution)/shard_map/hd,rh->dr/dot_general | solution.py:71
  124.7 1.0 convolution_convert_fusion
  125.7 3.9 %add_convert_fusion = bf16[6144,512]{1,0:T(8,128)(2,1)} fusion(bf16[6144,256]{1,0:T(8,128)(2,1)S(1)} %convolution_convert_fusion.2, bf16[6144,256]{1,0:T(8,128)(2,1)S(1)} %fusion, bf16[6144,256]{1,0:T(8,128)(2,1)S(1)} %convolution_convert_fusion, bf16[6144,256]{1,0:T(8,128)(2,1)S(1)} %fusion.1), kind=kLoop, calls=%fused_computation | loop fusion | flops 31457280 | bytes 18874368 | tf_op jit(solution)/shard_map/convert_element_type | solution.py:108
  129.6 0.8 copy-done.8
  130.5 3.1 %fusion.19 = f32[6144,128]{1,0:T(8,128)S(1)} fusion(bf16[256,128]{1,0:T(8,128)(2,1)S(1)} %copy-done.8, bf16[2,256,6144]{2,1,0:T(8,128)(2,1)} %all-gather.2.cloned.1.call-done), kind=kOutput, calls=%fused_computation.30 | convolution fusion | flops 402653184 | bytes 6356992 | tf_op jit(solution)/shard_map/rd,rh->dh/dot_general | solution.py:117
  133.5 0.1 collective-permute-start.3
  133.7 0.1 slice-done.1
  133.8 1.0 fusion.20
  134.8 0.7 collective-permute-start.2
  135.5 2.2 fusion.18
  137.7 0.1 collective-permute-start.4
  137.8 1.5 collective-permute-done.3
  139.3 2.2 fusion.6
  141.5 2.2 collective-permute-done.2
  143.8 2.2 fusion.7
  146.0 68.6 %reduce-scatter.2.cloned.1.call-done = bf16[384,512]{1,0:T(8,128)(2,1)} async-done(((bf16[6144,512]{1,0:T(8,128)(2,1)}), bf16[384,512]{1,0:T(8,128)(2,1)}) %reduce-scatter.2.cloned.1.call-update) | async-done | bytes 393232 | tf_op jit(solution)/shard_map/reduce_scatter | solution.py:109
  214.7 1.0 slice_bitcast_fusion.11
  215.7 0.2 copy.38
  215.9 0.2 copy.39
  216.0 0.8 pad_maximum_fusion.2
  216.8 7.5 %all-to-all-start.1 = ((bf16[8,64,384]{2,1,0:T(8,128)(2,1)}), bf16[8,64,384]{2,1,0:T(8,128)(2,1)S(1)}, u32[]{:S(2)}, u32[]{:S(2)}) async-start(bf16[8,64,384]{2,1,0:T(8,128)(2,1)} %pad_maximum_fusion.2), calls=%async_computation.2 | async-start | bytes 786432 | tf_op jit(solution)/shard_map/all_to_all | solution.py:130
  224.4 4.6 %fusion.5 = bf16[1,128,6144]{2,1,0:T(8,128)(2,1)} fusion(f32[128,6144]{1,0:T(8,128)} %collective-permute-done.4, bf16[256,128]{1,0:T(8,128)(2,1)S(1)} %get-tuple-element.10, bf16[2,256,6144]{2,1,0:T(8,128)(2,1)} %all-gather.2.cloned.1.call-done), kind=kOutput, calls=%fused_computation.13 | convolution fusion | flops 404226048 | bytes 7929856 | tf_op jit(solution)/shard_map/rh,rd->hd/dot_general | solution.py:118
  229.0 3.1 %all-to-all-done.1 = bf16[8,64,384]{2,1,0:T(8,128)(2,1)S(1)} async-done(((bf16[8,64,384]{2,1,0:T(8,128)(2,1)}), bf16[8,64,384]{2,1,0:T(8,128)(2,1)S(1)}, u32[]{:S(2)}, u32[]{:S(2)}) %all-to-all-start.1) | async-done | bytes 393248 | tf_op jit(solution)/shard_map/all_to_all | solution.py:130
  232.2 0.9 convolution_convert_fusion.7
  233.1 0.9 convolution_convert_fusion.6
  (45 shorter events, 0.3 us)
Async XLA Ops:
  7.2 2.6 %copy-start = (bf16[48,384]{1,0:T(8,128)(2,1)S(1)}, bf16[48,384]{1,0:T(8,128)(2,1)}, u32[]{:S(2)}) copy-start(bf16[48,384]{1,0:T(8,128)(2,1)} %param.13) | copy-start | bytes 110596
  7.2 20.6 %copy-start.5 = (bf16[1,6144,128]{2,1,0:T(8,128)(2,1)S(1)}, bf16[1,6144,128]{2,1,0:T(8,128)(2,1)}, u32[]{:S(2)}) copy-start(bf16[1,6144,128]{2,1,0:T(8,128)(2,1)} %param.10) | copy-start | bytes 4718596
  7.2 20.6 %copy-start.3 = (bf16[1,6144,128]{2,1,0:T(8,128)(2,1)S(1)}, bf16[1,6144,128]{2,1,0:T(8,128)(2,1)}, u32[]{:S(2)}) copy-start(bf16[1,6144,128]{2,1,0:T(8,128)(2,1)} %param.11) | copy-start | bytes 4718596
  7.2 103.4 %all-gather.2.cloned.1.call-start = ((), (), s32[]{:S(2)}) async-start(), calls=%async_computation.3 | async-start | bytes 6684672 | tf_op jit(solution)/shard_map/all_gather | solution.py:57
  9.7 1.3 copy-start.9
  27.8 186.9 %reduce-scatter.2.cloned.1.call-start = ((), (), s32[]{:S(2)}) async-start(), calls=%async_computation.4 | async-start | bytes 6684672 | tf_op jit(solution)/shard_map/reduce_scatter | solution.py:109
  28.2 5.7 %collective-permute-start = (bf16[6144,256]{1,0:T(8,128)(2,1)S(1)}, bf16[6144,256]{1,0:T(8,128)(2,1)S(1)}, u32[]{:S(2)}, u32[]{:S(2)}) collective-permute-start(bf16[6144,256]{1,0:T(8,128)(2,1)S(1)} %pad_maximum_fusion), channel_id=1, source_target_pairs={{0,16},{16,0},{1,17},{17,1},{2,18},{18,2},{3,19},{19,3},{4,20},{20... | collective-permute-start | bytes 9437192 | tf_op jit(solution)/shard_map/ppermute | solution.py:63
  28.3 87.1 %collective-permute-start.1 = (bf16[128,6144]{1,0:T(8,128)(2,1)}, bf16[128,6144]{1,0:T(8,128)(2,1)}, u32[]{:S(2)}, u32[]{:S(2)}) collective-permute-start(bf16[128,6144]{1,0:T(8,128)(2,1)} %bitcast.10), channel_id=1, source_target_pairs={{0,16},{16,0},{1,17},{17,1},{2,18},{18,2},{3,19},{19,3},{4,20},{20... | collective-permute-start | bytes 4718600 | tf_op jit(solution)/shard_map/ppermute | solution.py:63
  110.6 4.8 %copy-start.2 = (bf16[2,256,6144]{2,1,0:T(8,128)(2,1)S(1)}, bf16[2,256,6144]{2,1,0:T(8,128)(2,1)}, u32[]{:S(2)}) copy-start(bf16[2,256,6144]{2,1,0:T(8,128)(2,1)} %all-gather.2.cloned.1.call-done) | copy-start | bytes 18874372
  118.3 2.9 %copy-start.4 = (bf16[1,6144,128]{2,1,0:T(8,128)(2,1)S(1)}, bf16[1,6144,128]{2,1,0:T(8,128)(2,1)}, u32[]{:S(2)}) copy-start(bf16[1,6144,128]{2,1,0:T(8,128)(2,1)} %param.11) | copy-start | bytes 4718596
  118.3 2.9 %copy-start.6 = (bf16[1,6144,128]{2,1,0:T(8,128)(2,1)S(1)}, bf16[1,6144,128]{2,1,0:T(8,128)(2,1)}, u32[]{:S(2)}) copy-start(bf16[1,6144,128]{2,1,0:T(8,128)(2,1)} %param.10) | copy-start | bytes 4718596
  118.5 3.7 %copy-start.11 = (bf16[256,128]{1,0:T(8,128)(2,1)}, bf16[256,128]{1,0:T(8,128)(2,1)S(1)}, u32[]{:S(2)}) copy-start(bf16[256,128]{1,0:T(8,128)(2,1)S(1)} %get-tuple-element.8) | copy-start | bytes 196612
  118.5 3.7 %copy-start.13 = (bf16[256,128]{1,0:T(8,128)(2,1)}, bf16[256,128]{1,0:T(8,128)(2,1)S(1)}, u32[]{:S(2)}) copy-start(bf16[256,128]{1,0:T(8,128)(2,1)S(1)} %get-tuple-element.6) | copy-start | bytes 196612
  118.6 6.1 %copy-start.7 = (bf16[256,128]{1,0:T(8,128)(2,1)}, bf16[256,128]{1,0:T(8,128)(2,1)S(1)}, u32[]{:S(2)}) copy-start(bf16[256,128]{1,0:T(8,128)(2,1)S(1)} %get-tuple-element.7) | copy-start | bytes 196612
  129.6 0.8 copy-start.8
  129.6 4.0 %slice-start = ((s8[6291456]{0:T(1024)(128)(4,1)}), s8[2097152]{0:T(1024)(128)(4,1)S(1)}, s32[]{:S(2)}) async-start(s8[6291456]{0:T(1024)(128)(4,1)} %bitcast.62), calls=%async_computation.5 | async-start | bytes 4194304
  130.5 3.3 %slice-start.1 = ((s8[6291456]{0:T(1024)(128)(4,1)}), s8[4194304]{0:T(1024)(128)(4,1)S(1)}, s32[]{:S(2)}) async-start(s8[6291456]{0:T(1024)(128)(4,1)} %bitcast.62), calls=%async_computation.6 | async-start | bytes 8388608
  133.5 5.7 %collective-permute-start.3 = (f32[6144,128]{1,0:T(8,128)S(1)}, f32[6144,128]{1,0:T(8,128)S(1)}, u32[]{:S(2)}, u32[]{:S(2)}) collective-permute-start(f32[6144,128]{1,0:T(8,128)S(1)} %fusion.19), channel_id=1, source_target_pairs={{0,16},{16,0},{1,17},{17,1},{2,18},{18,2},{3,19},{19,3},{4,20},{20... | collective-permute-start | bytes 9437192 | tf_op jit(solution)/shard_map/ppermute | solution.py:122
  134.8 4.5 %copy-start.14 = (bf16[256,128]{1,0:T(8,128)(2,1)S(1)}, bf16[256,128]{1,0:T(8,128)(2,1)}, u32[]{:S(2)}) copy-start(bf16[256,128]{1,0:T(8,128)(2,1)} %copy-done.13) | copy-start | bytes 196612
  134.8 9.0 %collective-permute-start.2 = (f32[6144,128]{1,0:T(8,128)S(1)}, f32[6144,128]{1,0:T(8,128)S(1)}, u32[]{:S(2)}, u32[]{:S(2)}) collective-permute-start(f32[6144,128]{1,0:T(8,128)S(1)} %fusion.20), channel_id=1, source_target_pairs={{0,16},{16,0},{1,17},{17,1},{2,18},{18,2},{3,19},{19,3},{4,20},{20... | collective-permute-start | bytes 9437192 | tf_op jit(solution)/shard_map/ppermute | solution.py:122
  137.7 6.1 %copy-start.12 = (bf16[256,128]{1,0:T(8,128)(2,1)S(1)}, bf16[256,128]{1,0:T(8,128)(2,1)}, u32[]{:S(2)}) copy-start(bf16[256,128]{1,0:T(8,128)(2,1)} %copy-done.11) | copy-start | bytes 196612
  137.7 86.7 %collective-permute-start.4 = (f32[128,6144]{1,0:T(8,128)}, f32[128,6144]{1,0:T(8,128)}, u32[]{:S(2)}, u32[]{:S(2)}) collective-permute-start(f32[128,6144]{1,0:T(8,128)} %fusion.18), channel_id=1, source_target_pairs={{0,16},{16,0},{1,17},{17,1},{2,18},{18,2},{3,19},{19,3},{4,20},{20... | collective-permute-start | bytes 9437192 | tf_op jit(solution)/shard_map/ppermute | solution.py:122
  216.8 15.3 %all-to-all-start.1 = ((bf16[8,64,384]{2,1,0:T(8,128)(2,1)}), bf16[8,64,384]{2,1,0:T(8,128)(2,1)S(1)}, u32[]{:S(2)}, u32[]{:S(2)}) async-start(bf16[8,64,384]{2,1,0:T(8,128)(2,1)} %pad_maximum_fusion.2), calls=%async_computation.2 | async-start | bytes 786432 | tf_op jit(solution)/shard_map/all_to_all | solution.py:130
  224.4 8.7 %copy-start.10 = (f32[48,4,32]{0,2,1:T(8,128)S(1)}, f32[48,4,32]{0,2,1:T(8,128)}, u32[]{:S(2)}) copy-start(f32[48,4,32]{0,2,1:T(8,128)} %copy-done.9) | copy-start | bytes 73732
  224.4 9.6 %copy-start.1 = (bf16[48,384]{1,0:T(8,128)(2,1)S(1)}, bf16[48,384]{1,0:T(8,128)(2,1)}, u32[]{:S(2)}) copy-start(bf16[48,384]{1,0:T(8,128)(2,1)} %param.13) | copy-start | bytes 110596
Sparse Core Ops, SparseCore 0:
  27.9 82.6 all-gather.1
  129.8 84.8 reduce-scatter.1
where the time goes:
time: 241 us
  waiting for transfers between devices  157 us (65%)
  matrix products  33.3 us (14%)
  blocking collectives  15.8 us (7%)
  between operations  14.4 us (6%)
  starting transfers between devices  9.09 us (4%)
  other arithmetic  7.59 us (3%)
  local copies, waits for them, and re-layouts  3.4 us (1%)
    all_gather x1, waiting for transfers between devices, per_device(): mine_full = lax.all_gather(mine, TN, axis=2, tiled=True)  76.6 us
    reduce_scatter x1, waiting for transfers between devices, per_device(): scattered = lax.psum_scatter(summed, TN, scatter_dimension=0, tiled=True)  68.6 us
    all_to_all x1, blocking collectives, per_device(): recv = lax.all_to_all(send, SRC, split_axis=0, concat_axis=0, tiled=True)  15.8 us
    all_to_all x1, starting transfers between devices, per_device(): lax.all_to_all(done, SRC, split_axis=0, concat_axis=0, tiled=True)  7.54 us
    dot_general x2, matrix products, weight_grads(): jnp.einsum('rh,rd->hd', f[4], grads, preferred_element_type=jnp.float32)  6.88 us
    dot_general x2, matrix products, weight_grads(): jnp.einsum('rd,rh->dh', rows, b[1], preferred_element_type=jnp.float32)  5.32 us
    ppermute x2, waiting for transfers between devices, per_device(): gu_other, down_other = lax.ppermute((gu_local, down_local), 'core', pair)  5.15 us
    dot_general x2, matrix products, forward(): jnp.einsum('hd,rh->dr', down_w, hidden, preferred_element_type=jnp.float32)  5.07 us
  transfers between devices with their start and end apart: 8, of which 6 were waited for; matrix products, arithmetic and copies ran while one was open for 9% of the time, Pallas kernels for 0%

commit v1 on v0

--- a/solution.py
+++ b/solution.py
@@ -3,6 +3,7 @@
 from jax import lax
 from jax.experimental.layout import Layout, with_layout_constraint
 from jax.sharding import Mesh, NamedSharding, PartitionSpec as P
+from jax.lax import all_to_all, axis_size
 
 EXPERTS = 4
 CAP = 32
@@ -54,7 +55,9 @@
     recv = lax.all_to_all(send, SRC, split_axis=0, concat_axis=0, tiled=True)
     mine = recv.reshape(n_src, 2, CAP, feature_cols).transpose(1, 0, 2, 3)
     mine = mine.reshape(2, n_src * CAP, feature_cols)
-    mine_full = lax.all_gather(mine, TN, axis=2, tiled=True)
+    mine_full = jnp.concatenate(
+        all_to_all(jnp.stack([mine] * axis_size(TN)), TN, split_axis=0, concat_axis=0), axis=2
+    )
     pair = [(0, 1), (1, 0)]
     gate_local = gate_matrix[0]
     up_local = up_matrix[0]

time: 241 us -> 325 us (1.35)
  waiting for transfers between devices: 157 us -> 217 us
  local copies, waits for them, and re-layouts: 3.4 us -> 15.9 us
  starting transfers between devices: 9.09 us -> 16.5 us
    all_to_all x0 -> x1, waiting for transfers between devices: none -> 136 us  [per_device(): all_to_all(jnp.stack([mine] * axis_size(TN)), TN, split_axis=0, concat_ax...]
    all_gather x1 -> x0, waiting for transfers between devices: 76.6 us -> none  [per_device(): mine_full = lax.all_gather(mine, TN, axis=2, tiled=True)]
    all_to_all x0 -> x1, starting transfers between devices: none -> 8.9 us  [per_device(): all_to_all(jnp.stack([mine] * axis_size(TN)), TN, split_axis=0, concat_ax...]
    reduce_scatter x1, waiting for transfers between devices: 68.6 us -> 74.3 us  [per_device(): scattered = lax.psum_scatter(summed, TN, scatter_dimension=0, tiled=True)]
    ppermute x2, waiting for transfers between devices: 5.15 us -> 0.01 us  [per_device(): gu_other, down_other = lax.ppermute((gu_local, down_local), 'core', pair)]
    another operation x0 -> x2, local copies, waits for them, and re-layouts: none -> 3.52 us  [per_device(): jnp.stack([mine] * axis_size(TN))]
    dot_general x2, matrix products: 3.28 us -> 6.71 us  [weight_grads(): jnp.einsum('rd,rh->dh', rows, b[0], preferred_element_type=jnp.float32)]
  transfers between devices with their start and end apart: 8 -> 8, of which waited for: 6 -> 5; matrix products, arithmetic and copies ran while one was open for 9% -> 9% of each run, Pallas kernels for 0% -> 0%
where the time goes in v1:
time: 325 us; the launch traced here: 324 us
  waiting for transfers between devices  217 us (67%)
  matrix products  33.7 us (10%)
  starting transfers between devices  16.5 us (5%)
  local copies, waits for them, and re-layouts  15.9 us (5%)
  blocking collectives  15.8 us (5%)
  between operations  14.3 us (4%)
  other arithmetic  10.1 us (3%)
    all_to_all x1, waiting for transfers between devices, per_device(): all_to_all(jnp.stack([mine] * axis_size(TN)), TN, split_axis=0, concat_ax...  136 us
    reduce_scatter x1, waiting for transfers between devices, per_device(): scattered = lax.psum_scatter(summed, TN, scatter_dimension=0, tiled=True)  74.3 us
    all_to_all x1, blocking collectives, per_device(): recv = lax.all_to_all(send, SRC, split_axis=0, concat_axis=0, tiled=True)  15.8 us
    all_to_all x1, starting transfers between devices, per_device(): all_to_all(jnp.stack([mine] * axis_size(TN)), TN, split_axis=0, concat_ax...  8.9 us
    dot_general x2, matrix products, weight_grads(): jnp.einsum('rd,rh->dh', rows, b[0], preferred_element_type=jnp.float32)  6.71 us
  transfers between devices with their start and end apart: 8, of which 5 were waited for; matrix products, arithmetic and copies ran while one was open for 9% of the time, Pallas kernels for 0%

profile of v1, /device:TPU:8, one launch (start us, length us, event | category | flops | bytes accessed | tf_op | source)
XLA Modules:
  0.0 323.9 jit_solution(3678171571322285994)
XLA Ops:
  7.2 0.7 fusion.29
  7.9 0.1 copy.46
  8.0 0.1 reduce_window_sum.11
  8.1 0.1 copy.47
  8.1 0.7 convert_element_type.89
  8.8 0.7 select_reduce_fusion
  9.6 0.6 copy-done.9
  10.2 0.3 convolution_convert_fusion.5
  10.5 1.0 convolution_convert_fusion.4
  11.5 15.8 %all_to_all.15 = bf16[8,64,384]{2,1,0:T(8,128)(2,1)S(1)} all-to-all(bf16[8,64,384]{2,1,0:T(8,128)(2,1)S(1)} %pad_maximum_fusion.1), channel_id=1, replica_groups=mesh['y'=4,'xhi'=2,'core'=2,'xlo'=2,'z'=8] {'y','xhi'}, dimensions={0} | all-to-all | bytes 786432 | tf_op jit(solution)/shard_map/all_to_all | solution.py:55
  27.4 0.2 copy.49
  27.6 3.3 %stack.3 = bf16[16,2,256,384]{2,3,1,0:T(8,128)(2,1)} broadcast(bf16[2,256,384]{1,2,0:T(8,128)(2,1)S(1)} %copy.49), dimensions={1,2,3} | broadcast | bytes 6684672 | tf_op jit(solution)/shard_map/stack | solution.py:59
  30.9 8.9 %all-to-all-start.1 = ((bf16[16,2,256,384]{2,3,1,0:T(8,128)(2,1)}), bf16[16,2,256,384]{2,3,1,0:T(8,128)(2,1)}, u32[]{:S(2)}, u32[]{:S(2)}) async-start(bf16[16,2,256,384]{2,3,1,0:T(8,128)(2,1)} %stack.3), calls=%async_computation.1 | async-start | bytes 12582912 | tf_op jit(solution)/shard_map/all_to_all | solution.py:59
  39.9 2.0 pad_maximum_fusion
  41.9 0.5 collective-permute-start.1
  42.4 135.8 %all-to-all-done.1 = bf16[16,2,256,384]{2,3,1,0:T(8,128)(2,1)} async-done(((bf16[16,2,256,384]{2,3,1,0:T(8,128)(2,1)}), bf16[16,2,256,384]{2,3,1,0:T(8,128)(2,1)}, u32[]{:S(2)}, u32[]{:S(2)}) %all-to-all-start.1) | async-done | bytes 6291488 | tf_op jit(solution)/shard_map/all_to_all | solution.py:59
  178.2 3.2 copy.57
  181.4 0.4 fusion.35
  181.9 1.0 copy-done.5
  182.9 1.6 copy-done.7
  184.4 3.6 %fusion.8 = f32[256,512]{1,0:T(8,128)S(1)} fusion(bf16[256,6144]{0,1:T(8,128)(2,1)S(1)} %bitcast.63, bf16[6144,256]{1,0:T(8,128)(2,1)} %collective-permute-done, bf16[6144,128]{1,0:T(8,128)(2,1)S(1)} %bitcast.75, bf16[6144,128]{1,0:T(8,128)(2,1)S(1)} %bitcast.78), kind=kOutput, calls=%fused_computation.16 | convolution fusion | flops 1629487104 | bytes 9961472 | tf_op jit(solution)/shard_map/dot_general | solution.py:96
  188.1 3.0 fusion.14
  191.0 0.2 multiply_convert_fusion.1
  191.3 2.5 fusion
  193.8 1.0 convolution_convert_fusion.2
  194.8 2.4 fusion.1
  197.3 2.9 convolution_convert_fusion
  200.2 3.9 %add_convert_fusion = bf16[6144,512]{1,0:T(8,128)(2,1)} fusion(bf16[6144,256]{1,0:T(8,128)(2,1)S(1)} %convolution_convert_fusion.2, bf16[6144,256]{1,0:T(8,128)(2,1)S(1)} %fusion, bf16[6144,256]{1,0:T(8,128)(2,1)S(1)} %convolution_convert_fusion, bf16[6144,256]{1,0:T(8,128)(2,1)S(1)} %fusion.1), kind=kLoop, calls=%fused_computation | loop fusion | flops 31457280 | bytes 18874368 | tf_op jit(solution)/shard_map/convert_element_type | solution.py:111
  204.1 3.1 fusion.39
  207.2 0.1 collective-permute-start.4
  207.3 1.0 fusion.38
  208.3 0.6 collective-permute-start.3
  208.8 2.6 fusion.37
  211.5 1.4 collective-permute-done.4
  212.9 2.3 fusion.5
  215.2 2.2 collective-permute-done.3
  217.4 2.1 fusion.6
  219.5 74.3 %reduce-scatter.2.cloned.1.call-done = bf16[384,512]{1,0:T(8,128)(2,1)} async-done(((bf16[6144,512]{1,0:T(8,128)(2,1)}), bf16[384,512]{1,0:T(8,128)(2,1)}) %reduce-scatter.2.cloned.1.call-update) | async-done | bytes 393232 | tf_op jit(solution)/shard_map/reduce_scatter | solution.py:112
  293.8 1.7 slice_bitcast_fusion.1
  295.6 1.7 copy.53
  297.3 0.8 copy.54
  298.1 1.8 pad_maximum_fusion.2
  299.9 6.4 %all-to-all-start.2 = ((bf16[8,64,384]{2,1,0:T(8,128)(2,1)}), bf16[8,64,384]{2,1,0:T(8,128)(2,1)}, u32[]{:S(2)}, u32[]{:S(2)}) async-start(bf16[8,64,384]{2,1,0:T(8,128)(2,1)} %pad_maximum_fusion.2), calls=%async_computation.3 | async-start | bytes 786432 | tf_op jit(solution)/shard_map/all_to_all | solution.py:133
  306.3 4.1 %fusion.7 = bf16[1,6144,128]{2,1,0:T(8,128)(2,1)} fusion(f32[6144,128]{1,0:T(8,128)} %collective-permute-done.2, bf16[256,6144]{0,1:T(8,128)(2,1)S(1)} %bitcast.67, bf16[256,128]{1,0:T(8,128)(2,1)} %copy-done.11), kind=kOutput, calls=%fused_computation.15 | convolution fusion | flops 404226048 | bytes 7929856 | tf_op jit(solution)/shard_map/rd,rh->dh/dot_general | solution.py:119
  310.4 3.7 %all-to-all-done.2 = bf16[8,64,384]{2,1,0:T(8,128)(2,1)} async-done(((bf16[8,64,384]{2,1,0:T(8,128)(2,1)}), bf16[8,64,384]{2,1,0:T(8,128)(2,1)}, u32[]{:S(2)}, u32[]{:S(2)}) %all-to-all-start.2) | async-done | bytes 393248 | tf_op jit(solution)/shard_map/all_to_all | solution.py:133
  314.1 1.1 fusion.36
  315.2 0.9 convolution_convert_fusion.7
  316.1 0.9 convolution_convert_fusion.6
  (41 shorter events, 0.3 us)
Async XLA Ops:
  7.2 3.0 copy-start
  9.5 0.6 copy-start.9
  30.9 9.0 %copy-start.4 = (bf16[1,6144,128]{2,1,0:T(8,128)(2,1)S(1)}, bf16[1,6144,128]{2,1,0:T(8,128)(2,1)}, u32[]{:S(2)}) copy-start(bf16[1,6144,128]{2,1,0:T(8,128)(2,1)} %param.11) | copy-start | bytes 4718596
  30.9 9.0 %copy-start.6 = (bf16[1,6144,128]{2,1,0:T(8,128)(2,1)S(1)}, bf16[1,6144,128]{2,1,0:T(8,128)(2,1)}, u32[]{:S(2)}) copy-start(bf16[1,6144,128]{2,1,0:T(8,128)(2,1)} %param.10) | copy-start | bytes 4718596
  30.9 147.3 %all-to-all-start.1 = ((bf16[16,2,256,384]{2,3,1,0:T(8,128)(2,1)}), bf16[16,2,256,384]{2,3,1,0:T(8,128)(2,1)}, u32[]{:S(2)}, u32[]{:S(2)}) async-start(bf16[16,2,256,384]{2,3,1,0:T(8,128)(2,1)} %stack.3), calls=%async_computation.1 | async-start | bytes 12582912 | tf_op jit(solution)/shard_map/all_to_all | solution.py:59
  39.8 254.0 %reduce-scatter.2.cloned.1.call-start = ((), (), s32[]{:S(2)}) async-start(), calls=%async_computation.4 | async-start | bytes 6684672 | tf_op jit(solution)/shard_map/reduce_scatter | solution.py:112
  41.9 140.0 %collective-permute-start = (bf16[6144,256]{1,0:T(8,128)(2,1)}, bf16[6144,256]{1,0:T(8,128)(2,1)}, u32[]{:S(2)}, u32[]{:S(2)}) collective-permute-start(bf16[6144,256]{1,0:T(8,128)(2,1)} %pad_maximum_fusion), channel_id=1, source_target_pairs={{0,16},{16,0},{1,17},{17,1},{2,18},{18,2},{3,19},{19,3},{4,20},{20... | collective-permute-start | bytes 9437192 | tf_op jit(solution)/shard_map/ppermute | solution.py:66
  41.9 146.2 %collective-permute-start.1 = (bf16[128,6144]{1,0:T(8,128)(2,1)}, bf16[128,6144]{1,0:T(8,128)(2,1)}, u32[]{:S(2)}, u32[]{:S(2)}) collective-permute-start(bf16[128,6144]{1,0:T(8,128)(2,1)} %bitcast.11), channel_id=1, source_target_pairs={{0,16},{16,0},{1,17},{17,1},{2,18},{18,2},{3,19},{19,3},{4,20},{20... | collective-permute-start | bytes 4718600 | tf_op jit(solution)/shard_map/ppermute | solution.py:66
  181.4 1.5 copy-start.5
  181.4 3.0 copy-start.7
  181.9 6.2 %copy-start.2 = (bf16[1,256,16,384]{1,3,2,0:T(8,128)(2,1)}, bf16[1,256,16,384]{1,3,2,0:T(8,128)(2,1)S(1)}, u32[]{:S(2)}) copy-start(bf16[1,256,16,384]{1,3,2,0:T(8,128)(2,1)S(1)} %get-tuple-element.6) | copy-start | bytes 9437188
  191.2 3.6 %copy-start.11 = (bf16[256,128]{1,0:T(8,128)(2,1)}, bf16[256,128]{1,0:T(8,128)(2,1)S(1)}, u32[]{:S(2)}) copy-start(bf16[256,128]{1,0:T(8,128)(2,1)S(1)} %get-tuple-element.10) | copy-start | bytes 196612
  191.2 3.6 %copy-start.12 = (bf16[256,128]{1,0:T(8,128)(2,1)}, bf16[256,128]{1,0:T(8,128)(2,1)S(1)}, u32[]{:S(2)}) copy-start(bf16[256,128]{1,0:T(8,128)(2,1)S(1)} %get-tuple-element.8) | copy-start | bytes 196612
  191.3 3.6 %copy-start.8 = (bf16[256,128]{1,0:T(8,128)(2,1)}, bf16[256,128]{1,0:T(8,128)(2,1)S(1)}, u32[]{:S(2)}) copy-start(bf16[256,128]{1,0:T(8,128)(2,1)S(1)} %get-tuple-element.11) | copy-start | bytes 196612
  207.2 5.7 %collective-permute-start.4 = (f32[128,6144]{1,0:T(8,128)S(1)}, f32[128,6144]{1,0:T(8,128)S(1)}, u32[]{:S(2)}, u32[]{:S(2)}) collective-permute-start(f32[128,6144]{1,0:T(8,128)S(1)} %fusion.39), channel_id=1, source_target_pairs={{0,16},{16,0},{1,17},{17,1},{2,18},{18,2},{3,19},{19,3},{4,20},{20... | collective-permute-start | bytes 9437192 | tf_op jit(solution)/shard_map/ppermute | solution.py:125
  208.3 4.7 %copy-start.3 = (bf16[1,256,16,384]{1,3,2,0:T(8,128)(2,1)S(1)}, bf16[1,256,16,384]{1,3,2,0:T(8,128)(2,1)}, u32[]{:S(2)}) copy-start(bf16[1,256,16,384]{1,3,2,0:T(8,128)(2,1)} %copy-done.2) | copy-start | bytes 9437188
  208.3 9.2 %collective-permute-start.3 = (f32[6144,128]{1,0:T(8,128)S(1)}, f32[6144,128]{1,0:T(8,128)S(1)}, u32[]{:S(2)}, u32[]{:S(2)}) collective-permute-start(f32[6144,128]{1,0:T(8,128)S(1)} %fusion.38), channel_id=1, source_target_pairs={{0,16},{16,0},{1,17},{17,1},{2,18},{18,2},{3,19},{19,3},{4,20},{20... | collective-permute-start | bytes 9437192 | tf_op jit(solution)/shard_map/ppermute | solution.py:125
  211.5 5.9 %copy-start.13 = (bf16[256,128]{1,0:T(8,128)(2,1)S(1)}, bf16[256,128]{1,0:T(8,128)(2,1)}, u32[]{:S(2)}) copy-start(bf16[256,128]{1,0:T(8,128)(2,1)} %copy-done.12) | copy-start | bytes 196612
  211.5 94.8 %collective-permute-start.2 = (f32[6144,128]{1,0:T(8,128)}, f32[6144,128]{1,0:T(8,128)}, u32[]{:S(2)}, u32[]{:S(2)}) collective-permute-start(f32[6144,128]{1,0:T(8,128)} %fusion.37), channel_id=1, source_target_pairs={{0,16},{16,0},{1,17},{17,1},{2,18},{18,2},{3,19},{19,3},{4,20},{20... | collective-permute-start | bytes 9437192 | tf_op jit(solution)/shard_map/ppermute | solution.py:125
  299.9 14.2 %all-to-all-start.2 = ((bf16[8,64,384]{2,1,0:T(8,128)(2,1)}), bf16[8,64,384]{2,1,0:T(8,128)(2,1)}, u32[]{:S(2)}, u32[]{:S(2)}) async-start(bf16[8,64,384]{2,1,0:T(8,128)(2,1)} %pad_maximum_fusion.2), calls=%async_computation.3 | async-start | bytes 786432 | tf_op jit(solution)/shard_map/all_to_all | solution.py:133
  306.3 9.8 %copy-start.10 = (f32[48,4,32]{0,2,1:T(8,128)S(1)}, f32[48,4,32]{0,2,1:T(8,128)}, u32[]{:S(2)}) copy-start(f32[48,4,32]{0,2,1:T(8,128)} %copy-done.9) | copy-start | bytes 73732
  306.3 10.7 %copy-start.1 = (bf16[48,384]{1,0:T(8,128)(2,1)S(1)}, bf16[48,384]{1,0:T(8,128)(2,1)}, u32[]{:S(2)}) copy-start(bf16[48,384]{1,0:T(8,128)(2,1)} %param.13) | copy-start | bytes 110596
Sparse Core Ops, SparseCore 0:
  204.2 89.5 reduce-scatter.1
